TPU v7x, 32 devices: a whole 2x2x4 slice. The times are simulated.
32 devices in a mesh: groups: 2 (over y), seq: 4 (over x, core), fsdp: 4 (over z).
Axes of the slice: x: 2, y: 2, z: 4, core: 2. Of those that a mesh axis runs over, the one named last changes fastest.
Arguments:
- tokens: bfloat16 [16, 512, 1536], P(('groups', 'fsdp'), 'seq'), parts along dimension 0, may hold values from -6 to 6
- in_weight: bfloat16 [1536, 4608], P(None, 'fsdp'), may hold values from -0.15625 to 0.15625
- short_weight: float32 [3, 4608], replicated, may hold values from -3.5 to 3.5
- basis_in: float32 [17, 64], replicated, may hold values from -4 to 4
- basis_bias: float32 [64], replicated, may hold values from -3.140625 to 3.140625
- basis_mid: float32 [64, 64], replicated, may hold values from -1.5 to 1.5
- basis_shift: float32 [64], replicated, may hold values from -3.140625 to 3.140625
- response_out: float32 [2, 64, 1536], P(None, None, 'fsdp'), may hold values from -0.0234375 to 0.0234375
- skip_gain: float32 [1536], P('fsdp'), may hold values from -4 to 4
- block_counts: int32 [16, 4], P(('groups', 'fsdp'), 'seq'), parts along dimension 0, may hold values from 1 to 128, as said below
Outputs:
- mixed: bfloat16 [16, 512, 1536], P(('groups', 'fsdp'), 'seq'), parts along dimension 0
There are 2 independent parts, one for each index of `groups`. A program takes and returns all parts, laid end to end along the dimension named above; an argument that names none is the same for every part. Nothing has to cross between parts.
Inputs may be any that keep to these rules, and one draw needn't show every extreme that they name: `block_counts`: in every table one block holds all 128 tokens and another holds a single token.
All inputs are finite; a program needn't handle non-finite values.
Results may differ from a plain program's by a relative error of at most 0.007.
Values may be sent and summed in bfloat16 or wider, within the bound.
No kernel may reach another device: no remote copies, remote signals or barrier semaphores. Data moves between devices by JAX's collectives and lax.ppermute only.
A program may use at most 128 MiB of HBM per device.

v0:
```python
import jax
import jax.numpy as jnp
from jax import lax
from jax.sharding import PartitionSpec as P


def padded_2(cells, sides, width):
    for axis, dim in sides:
        count = lax.axis_size(axis)
        ends = count - 1
        head = lax.slice_in_dim(cells, 0, width, axis=dim)
        tail = lax.slice_in_dim(cells, cells.shape[dim] - width, cells.shape[dim], axis=dim)
        cells = jnp.concatenate(
            [
                lax.ppermute(tail, axis, [(i, (i + 1) % count) for i in range(ends)]),
                cells,
                lax.ppermute(head, axis, [((i + 1) % count, i) for i in range(ends)]),
            ],
            axis=dim,
        )
    return cells


def filter_basis(lag_values, total_len, basis_in, basis_bias, basis_mid, basis_shift):
    band_count = (basis_in.shape[0] - 1) // 2
    distance = jnp.abs(lag_values)
    periods = (2 ** (jnp.arange(band_count, dtype=jnp.int32) + 2) + 1).astype(jnp.int32)
    angles = (
        2.0
        * jnp.pi
        * (distance[:, None] % periods[None, :]).astype(jnp.float32)
        / periods[None, :].astype(jnp.float32)
    )
    linear = distance.astype(jnp.float32)[:, None] / total_len
    encoded = jnp.concatenate([linear, jnp.cos(angles), jnp.sin(angles)], axis=1)
    hidden = jnp.sin(jnp.dot(encoded, basis_in, precision=lax.Precision.HIGHEST) + basis_bias)
    return jnp.sin(jnp.dot(hidden, basis_mid, precision=lax.Precision.HIGHEST) + basis_shift)


def forward_table(block_len):
    period = 2 * block_len
    frequency = jnp.arange(block_len, dtype=jnp.int32)[:, None]
    samples = jnp.arange(period, dtype=jnp.int32)[None, :]
    phases = 2.0 * jnp.pi / period * (frequency * samples % period).astype(jnp.float32)
    alternate = (1 - 2 * (samples % 2)).astype(jnp.float32)
    real_rows = jnp.cos(phases)
    imag_rows = jnp.where(frequency == 0, alternate, -jnp.sin(phases))
    return jnp.concatenate([real_rows, imag_rows], axis=0)


def inverse_table(block_len):
    period = 2 * block_len
    places = jnp.arange(block_len, dtype=jnp.int32)[:, None]
    frequency = jnp.arange(block_len, dtype=jnp.int32)[None, :]
    phases = 2.0 * jnp.pi / period * (places * frequency % period).astype(jnp.float32)
    alternate = (1 - 2 * (places % 2)).astype(jnp.float32)
    real_cols = jnp.where(frequency == 0, 1.0, 2.0 * jnp.cos(phases)) / period
    imag_cols = jnp.where(frequency == 0, alternate, -2.0 * jnp.sin(phases)) / period
    return jnp.concatenate([real_cols, imag_cols], axis=1)


def packed_product(response, signal, block_len):
    first_slot = (jnp.arange(block_len) == 0)[:, None]
    resp_real = response[..., :block_len, :]
    resp_imag = response[..., block_len:, :]
    sig_real = signal[..., :block_len, :]
    sig_imag = signal[..., block_len:, :]
    cross_term = resp_imag * sig_imag
    prod_real = resp_real * sig_real - jnp.where(first_slot, 0.0, cross_term)
    prod_imag = jnp.where(first_slot, cross_term, resp_real * sig_imag + resp_imag * sig_real)
    return jnp.concatenate([prod_real, prod_imag], axis=-2)


def shards(
    tokens,
    in_weight,
    short_weight,
    basis_in,
    basis_bias,
    basis_mid,
    basis_shift,
    response_out,
    skip_gain,
    block_counts,
):
    seq_dev, block_len, width = tokens.shape
    group_tokens = lax.all_gather(tokens, "fsdp", axis=0, tiled=True)
    group_rows = group_tokens.shape[0]
    local_cols = in_weight.shape[1]
    partial = jnp.dot(
        group_tokens.reshape(group_rows * block_len, width),
        in_weight,
        preferred_element_type=jnp.float32,
    ).astype(jnp.bfloat16)
    partial = partial.reshape(group_rows, block_len, local_cols)
    projected = lax.all_to_all(partial, "fsdp", 0, 2, tiled=True)
    padded = padded_2(projected, (("seq", 1),), 1)
    shorted = (
        short_weight[0] * padded[:, :-2]
        + short_weight[1] * padded[:, 1:-1]
        + short_weight[2] * padded[:, 2:]
    )
    query_gate = shorted[:, :, :width]
    key_part = shorted[:, :, width : 2 * width]
    value_part = shorted[:, :, 2 * width :]
    valid_mask = (jnp.arange(block_len, dtype=jnp.int32)[None, :] < block_counts).astype(
        jnp.float32
    )
    carried = (key_part * value_part * valid_mask[:, :, None]).astype(jnp.bfloat16)
    full_out, full_skip = (
        lax.all_gather(response_out, "fsdp", axis=2, tiled=True),
        lax.all_gather(skip_gain, "fsdp", axis=0, tiled=True),
    )
    stacked_out = full_out.reshape(2 * full_out.shape[1], width)
    seq_count = lax.axis_size("seq")
    position = lax.axis_index("seq")
    total_len = float(seq_count * block_len)
    forward = forward_table(block_len)
    forward_half = forward[:, :block_len]
    inverse = inverse_table(block_len)
    circular = jnp.arange(2 * block_len, dtype=jnp.int32)
    wrapped = jnp.where(circular < block_len, circular, circular - 2 * block_len)

    def kernel_response(offset, out_cols):
        lag_values = offset + wrapped
        basis_rows = filter_basis(
            lag_values, total_len, basis_in, basis_bias, basis_mid, basis_shift
        )
        ahead_mask = (lag_values >= 0).astype(jnp.float32)[:, None]
        paired = jnp.concatenate([basis_rows * ahead_mask, basis_rows * (1.0 - ahead_mask)], axis=1)
        return jnp.dot(
            jnp.dot(forward, paired, precision=lax.Precision.HIGHEST),
            out_cols,
            precision=lax.Precision.HIGHEST,
        )

    def add_block(spectrum, block_rows, start):
        offset = position * block_len - start
        response = kernel_response(offset, stacked_out)
        signal = jnp.einsum(
            "fc,scd->sfd",
            forward_half,
            block_rows.astype(jnp.float32),
            precision=lax.Precision.HIGHEST,
        )
        return spectrum + packed_product(response[None], signal, block_len)

    initial = jnp.zeros((seq_dev, 2 * block_len, width), jnp.float32)
    piece = lax.all_gather(carried, "seq", axis=1, tiled=True)
    piece_rows = piece.shape[1]
    block_total = piece_rows // block_len

    def one_block(block_index, carry):
        block_rows = lax.dynamic_slice_in_dim(piece, block_index * block_len, block_len, 1)
        return add_block(carry, block_rows, block_index * block_len)

    spectrum = lax.fori_loop(0, block_total, one_block, initial)
    conv = jnp.einsum("if,sfd->sid", inverse, spectrum, precision=lax.Precision.HIGHEST)
    return (query_gate * (conv + full_skip * carried.astype(jnp.float32))).astype(jnp.bfloat16)


def solution(mesh):
    placed = (
        P(("groups", "fsdp"), "seq", None),
        P(None, "fsdp"),
        P(),
        P(),
        P(),
        P(),
        P(),
        P(None, None, "fsdp"),
        P("fsdp"),
        P(("groups", "fsdp"), "seq"),
    )
    return jax.shard_map(
        shards,
        mesh=mesh,
        in_specs=placed,
        out_specs=P(("groups", "fsdp"), "seq", None),
        check_vma=False,
    )
```

profile of v0, /device:TPU:2, one launch (start us, length us, event | category | flops | bytes accessed | tf_op | source)
XLA Modules:
  0.0 302.2 jit_solution(2501134679842409714)
XLA Ops:
  6.5 0.7 all-gather.4.cloned.1.call-update
  7.3 66.4 %all-gather.4.cloned.1.call-done = bf16[8,128,1536]{2,1,0:T(8,128)(2,1)} async-done(((bf16[2,128,1536]{2,1,0:T(8,128)(2,1)}), bf16[8,128,1536]{2,1,0:T(8,128)(2,1)}) %all-gather.4.cloned.1.call-update) | async-done | bytes 3145744 | tf_op jit(solution)/shard_map/all_gather | solution.py:87
  73.7 7.6 %convolution_convert_fusion = bf16[1024,1152]{1,0:T(8,128)(2,1)} fusion(bf16[1024,1536]{1,0:T(8,128)(2,1)} %bitcast.65, bf16[1536,1152]{1,0:T(8,128)(2,1)S(1)} %copy-done), kind=kOutput, calls=%fused_computation.58 | convolution fusion | flops 3625058304 | bytes 9043968 | tf_op jit(solution)/shard_map/dot_general | solution.py:90
  81.3 4.6 %all-to-all-start = ((bf16[8,128,1152]{2,1,0:T(8,128)(2,1)}), bf16[8,128,1152]{2,1,0:T(8,128)(2,1)}, u32[]{:S(2)}, u32[]{:S(2)}) async-start(bf16[8,128,1152]{2,1,0:T(8,128)(2,1)} %bitcast.63), calls=%async_computation | async-start | bytes 4718592 | tf_op jit(solution)/shard_map/all_to_all | solution.py:96
  85.9 0.0 all-gather.6.cloned.1.call-start
  86.0 0.1 compare_convert_fusion.1
  86.0 54.0 %all-to-all-done = bf16[8,128,1152]{2,1,0:T(8,128)(2,1)} async-done(((bf16[8,128,1152]{2,1,0:T(8,128)(2,1)}), bf16[8,128,1152]{2,1,0:T(8,128)(2,1)}, u32[]{:S(2)}, u32[]{:S(2)}) %all-to-all-start) | async-done | bytes 2359328 | tf_op jit(solution)/shard_map/all_to_all | solution.py:96
  140.0 4.3 %copy.20 = bf16[4,2,128,1152]{2,3,0,1:T(8,128)(2,1)} copy(bf16[4,2,128,1152]{3,2,1,0:T(8,128)(2,1)} %bitcast.2) | data formatting | bytes 4718592 | tf_op jit(solution)/shard_map/all_to_all | solution.py:96
  144.3 5.3 %fusion.56 = (bf16[2,1,4608]{1,2,0:T(8,128)(2,1)}, bf16[2,1,4608]{1,2,0:T(8,128)(2,1)}) fusion(bf16[2,128,4608]{1,2,0:T(8,128)(2,1)} %bitcast.60), kind=kLoop, calls=%fused_computation.111 | loop fusion | bytes 73728 | tf_op jit(solution)/shard_map/slice | solution.py:12
  149.6 2.7 copy.21
  152.3 1.9 collective-permute-start
  154.2 2.7 copy.23
  156.9 3.6 %collective-permute-start.1 = (bf16[2,1,4608]{2,0,1:T(2,128)(2,1)}, bf16[2,1,4608]{2,0,1:T(2,128)(2,1)}, u32[]{:S(2)}, u32[]{:S(2)}) collective-permute-start(bf16[2,1,4608]{2,0,1:T(2,128)(2,1)} %copy.23), channel_id=1, source_target_pairs={{4,0},{8,4},{12,8},{5,1},{9,5},{13,9},{6,2},{10,6},{14,10},{7,3},{... | collective-permute-start | bytes 55304 | tf_op jit(solution)/shard_map/ppermute | solution.py:17
  160.5 1.8 slice_reduce_fusion.2
  162.3 2.6 copy.22
  164.9 2.6 copy.24
  167.6 7.7 %multiply_add_fusion = f32[2,128,4608]{1,2,0:T(8,128)S(1)} fusion(bf16[2,128,4608]{1,2,0:T(8,128)(2,1)} %bitcast.61, bf16[2,1,4608]{1,2,0:T(8,128)(2,1)} %copy.24, bf16[2,1,4608]{1,2,0:T(8,128)(2,1)} %copy.22, f32[4608]{0:T(1024)} %get-tuple-element.353, f32[4608]{0:T(1024)} %get-tuple-element.354, f32[4608]{0:T(1024)} %get-tuple-element.352), kind=kLoop, calls=%fused_computation.57 | loop fusion | flops 16515072 | bytes 7170048 | tf_op jit(solution)/shard_map/add | solution.py:99
  175.3 2.1 copy-done.3
  177.4 1.0 fusion.31
  178.5 11.9 %all-gather = f32[4,1,384]{2,1,0:T(1,128)S(1)} all-gather(f32[1,1,384]{2,1,0:T(1,128)S(1)} %reshape.183), channel_id=1, replica_groups=mesh['groups'=2,'seq'=4,'fsdp'=4] {'fsdp'}, dimensions={0}, use_global_device_ids=true | all-gather | bytes 7680 | tf_op jit(solution)/shard_map/all_gather | solution.py:112
  190.4 0.5 negate_select_fusion.2
  191.0 0.7 fusion.36
  191.6 0.7 pad_maximum_fusion.2
  192.4 0.9 select_multiply_fusion.1
  193.3 18.5 %all_gather.13 = f32[2,64,1536]{2,1,0:T(8,128)} all-gather(f32[2,64,384]{2,1,0:T(8,128)} %param.19), channel_id=1, replica_groups=mesh['groups'=2,'seq'=4,'fsdp'=4] {'fsdp'}, dimensions={2}, use_global_device_ids=true | all-gather | bytes 983040 | tf_op jit(solution)/shard_map/all_gather | solution.py:111
  211.8 72.5 %while.16 = (s32[]{:T(128)}, f32[2,256,1536]{2,1,0:T(8,128)}, s32[]{:T(128)}, f32[17,64]{1,0:T(8,128)}, f32[64]{0:T(128)}, /*index=5*/f32[64,64]{1,0:T(8,128)}, ...) while((s32[]{:T(128)}, f32[2,256,1536]{2,1,0:T(8,128)}, ...), condition=%wide.region_1.2_spmd.clone, body=%wide.region_0.1_spmd.clone.sunk | while | flops 1934166400 | bytes 34141608 | solution.py:157
  211.9 0.2 fusion.91
  212.2 1.2 fusion.92
  213.4 1.2 broadcast_multiply_fusion.3
  214.6 1.3 fusion.93
  216.0 2.6 convolution_bitcast_fusion.6
  218.5 1.3 slice_bitcast_fusion.3
  219.8 2.7 convolution_bitcast_fusion.5
  222.5 2.5 select_subtract_fusion.2
  225.0 4.3 %maximum_add_fusion.2 = f32[2,256,1536]{2,1,0:T(8,128)} fusion(f32[2,128,1536]{2,1,0:T(8,128)} %get-tuple-element.484, f32[2,128,1536]{2,1,0:T(8,128)} %get-tuple-element.485, f32[2,256,1536]{2,1,0:T(8,128)} %get-tuple-element.502, pred[]{:T(512)S(6)} %compare.7), kind=kLoop, calls=%fused_computation.2.clone.1 | loop fusion | flops 2359296 | bytes 9437185 | tf_op jit(solution)/shard_map/while/body/eval_jaxpr/add | solution.py:146
  229.3 0.2 fusion.91
  229.6 1.2 fusion.92
  230.8 1.2 broadcast_multiply_fusion.3
  232.0 1.4 fusion.93
  233.4 2.6 convolution_bitcast_fusion.6
  235.9 1.3 slice_bitcast_fusion.3
  237.2 2.7 convolution_bitcast_fusion.5
  239.9 2.5 select_subtract_fusion.2
  242.4 5.2 %maximum_add_fusion.2 = f32[2,256,1536]{2,1,0:T(8,128)} fusion(f32[2,128,1536]{2,1,0:T(8,128)} %get-tuple-element.484, f32[2,128,1536]{2,1,0:T(8,128)} %get-tuple-element.485, f32[2,256,1536]{2,1,0:T(8,128)} %get-tuple-element.502, pred[]{:T(512)S(6)} %compare.7), kind=kLoop, calls=%fused_computation.2.clone.1 | loop fusion | flops 2359296 | bytes 9437185 | tf_op jit(solution)/shard_map/while/body/eval_jaxpr/add | solution.py:146
  247.6 0.2 fusion.91
  247.9 1.2 fusion.92
  249.1 1.2 broadcast_multiply_fusion.3
  250.4 1.3 fusion.93
  251.7 2.6 convolution_bitcast_fusion.6
  254.3 1.3 slice_bitcast_fusion.3
  255.6 2.7 convolution_bitcast_fusion.5
  258.3 2.5 select_subtract_fusion.2
  260.7 5.2 %maximum_add_fusion.2 = f32[2,256,1536]{2,1,0:T(8,128)} fusion(f32[2,128,1536]{2,1,0:T(8,128)} %get-tuple-element.484, f32[2,128,1536]{2,1,0:T(8,128)} %get-tuple-element.485, f32[2,256,1536]{2,1,0:T(8,128)} %get-tuple-element.502, pred[]{:T(512)S(6)} %compare.7), kind=kLoop, calls=%fused_computation.2.clone.1 | loop fusion | flops 2359296 | bytes 9437185 | tf_op jit(solution)/shard_map/while/body/eval_jaxpr/add | solution.py:146
  266.0 0.2 fusion.91
  266.3 1.2 fusion.92
  267.5 1.2 broadcast_multiply_fusion.3
  268.7 1.3 fusion.93
  270.1 2.6 convolution_bitcast_fusion.6
  272.6 1.3 slice_bitcast_fusion.3
  273.9 2.7 convolution_bitcast_fusion.5
  276.6 2.5 select_subtract_fusion.2
  279.1 5.2 %maximum_add_fusion.2 = f32[2,256,1536]{2,1,0:T(8,128)} fusion(f32[2,128,1536]{2,1,0:T(8,128)} %get-tuple-element.484, f32[2,128,1536]{2,1,0:T(8,128)} %get-tuple-element.485, f32[2,256,1536]{2,1,0:T(8,128)} %get-tuple-element.502, pred[]{:T(512)S(6)} %compare.7), kind=kLoop, calls=%fused_computation.2.clone.1 | loop fusion | flops 2359296 | bytes 9437185 | tf_op jit(solution)/shard_map/while/body/eval_jaxpr/add | solution.py:146
  284.3 8.8 %fusion.32 = bf16[2,128,1536]{1,2,0:T(8,128)(2,1)} fusion(f32[2,128,4608]{1,2,0:T(8,128)} %copy-done.3, f32[2,256,1536]{2,1,0:T(8,128)} %get-tuple-element.280, bf16[2,128,1536]{1,2,0:T(8,128)(2,1)} %fusion.31, f32[1536]{0:T(1024)S(1)} %reshape.184, f32[128,128]{1,0:T(8,128)} %get-tuple-element.392, f32[128,128]{1,0:T(8,128)} %get-tuple-element.391), kind=kOutput, calls=%fused_computation.67 | convolution fusion | flops 1209958400 | bytes 6428672 | tf_op jit(solution)/shard_map/if,sfd->sid/dot_general | solution.py:158
  293.1 2.3 copy.27
  (59 shorter events, 0.4 us)
Async XLA Ops:
  6.5 67.2 %copy-start = (bf16[1536,1152]{1,0:T(8,128)(2,1)S(1)}, bf16[1536,1152]{1,0:T(8,128)(2,1)}, u32[]{:S(2)}) copy-start(bf16[1536,1152]{1,0:T(8,128)(2,1)} %param.13) | copy-start | bytes 10616836
  6.5 67.2 %all-gather.4.cloned.1.call-start = ((), (), s32[]{:S(2)}) async-start(), calls=%async_computation.1 | async-start | bytes 3932160 | tf_op jit(solution)/shard_map/all_gather | solution.py:87
  81.3 4.7 %copy-start.5 = (s32[2,1]{0,1:T(1,128)S(1)}, s32[2,1]{0,1:T(1,128)}, u32[]{:S(2)}) copy-start(s32[2,1]{0,1:T(1,128)} %param.21) | copy-start | bytes 28
  81.3 58.8 %all-to-all-start = ((bf16[8,128,1152]{2,1,0:T(8,128)(2,1)}), bf16[8,128,1152]{2,1,0:T(8,128)(2,1)}, u32[]{:S(2)}, u32[]{:S(2)}) async-start(bf16[8,128,1152]{2,1,0:T(8,128)(2,1)} %bitcast.63), calls=%async_computation | async-start | bytes 4718592 | tf_op jit(solution)/shard_map/all_to_all | solution.py:96
  85.9 125.9 %all-gather.6.cloned.1.call-start = ((), (), s32[]{:S(2)}) async-start(), calls=%async_computation.2 | async-start | bytes 3932160 | tf_op jit(solution)/shard_map/all_gather | solution.py:149
  152.3 10.0 %collective-permute-start = (bf16[2,1,4608]{2,0,1:T(2,128)(2,1)}, bf16[2,1,4608]{2,0,1:T(2,128)(2,1)}, u32[]{:S(2)}, u32[]{:S(2)}) collective-permute-start(bf16[2,1,4608]{2,0,1:T(2,128)(2,1)} %copy.21), channel_id=1, source_target_pairs={{0,4},{4,8},{8,12},{1,5},{5,9},{9,13},{2,6},{6,10},{10,14},{3,7},{... | collective-permute-start | bytes 55304 | tf_op jit(solution)/shard_map/ppermute | solution.py:15
  156.9 8.0 %collective-permute-start.1 = (bf16[2,1,4608]{2,0,1:T(2,128)(2,1)}, bf16[2,1,4608]{2,0,1:T(2,128)(2,1)}, u32[]{:S(2)}, u32[]{:S(2)}) collective-permute-start(bf16[2,1,4608]{2,0,1:T(2,128)(2,1)} %copy.23), channel_id=1, source_target_pairs={{4,0},{8,4},{12,8},{5,1},{9,5},{13,9},{6,2},{10,6},{14,10},{7,3},{... | collective-permute-start | bytes 55304 | tf_op jit(solution)/shard_map/ppermute | solution.py:17
  175.2 2.1 copy-start.3
  177.4 1.1 copy-start.4
  219.8 2.7 copy-start.1
  219.8 2.7 copy-start.2
  237.2 2.7 copy-start.1
  237.2 2.7 copy-start.2
  255.6 2.7 copy-start.1
  255.6 2.7 copy-start.2
  273.9 2.7 copy-start.1
  273.9 2.7 copy-start.2
Sparse Core Ops, SparseCore 0:
  8.9 64.7 all-gather.3
  178.6 26.8 all-gather.5
where the time goes:
time: 304 us; the launch traced here: 302 us
  waiting for transfers between devices  121 us (40%)
  matrix products  52.3 us (17%)
  other arithmetic  42.7 us (14%)
  local copies, waits for them, and re-layouts  31.5 us (10%)
  blocking collectives  30.4 us (10%)
  between operations  13.5 us (4%)
  starting transfers between devices  10.2 us (3%)
    all_gather x1, waiting for transfers between devices, shards(): group_tokens = lax.all_gather(tokens, 'fsdp', axis=0, tiled=True)  66.4 us
    all_to_all x1, waiting for transfers between devices, shards(): projected = lax.all_to_all(partial, 'fsdp', 0, 2, tiled=True)  54 us
    add x4, other arithmetic, add_block(): return spectrum + packed_product(response[None], signal, block_len)  19.9 us
    all_gather x1, blocking collectives, shards(): lax.all_gather(response_out, 'fsdp', axis=2, tiled=True)  18.5 us
    all_gather x1, blocking collectives, shards(): lax.all_gather(skip_gain, 'fsdp', axis=0, tiled=True)  11.9 us
    dot_general x4, matrix products, add_block(): jnp.einsum('fc,scd->sfd', forward_half, block_rows.astype(jnp.float32), p...  10.7 us
    dot_general x4, matrix products, kernel_response(): jnp.dot(jnp.dot(forward, paired, precision=lax.Precision.HIGHEST), out_co...  10.3 us
    sub x4, other arithmetic, packed_product(): prod_real = resp_real * sig_real - jnp.where(first_slot, 0.0, cross_term)  9.89 us
  transfers between devices with their start and end apart: 5, of which 2 were waited for; matrix products, arithmetic and copies ran while one was open for 3% of the time, Pallas kernels for 0%

commit v1 on v0

--- a/solution.py
+++ b/solution.py
@@ -2,6 +2,13 @@
 import jax.numpy as jnp
 from jax import lax
 from jax.sharding import PartitionSpec as P
+
+
+def wait_gates(shard_in, out_dim):
+    mixed_arr = list(shard_in.shape[1:])
+    mixed_arr[out_dim] *= shard_in.shape[0]
+    local_out = jnp.moveaxis(shard_in, 0, out_dim).reshape(mixed_arr)
+    return local_out
 
 
 def padded_2(cells, sides, width):
@@ -84,7 +91,25 @@
     block_counts,
 ):
     seq_dev, block_len, width = tokens.shape
-    group_tokens = lax.all_gather(tokens, "fsdp", axis=0, tiled=True)
+    count_all = lax.psum(1, axis_name="fsdp")
+    vals = tuple(((dev_j, (dev_j + 1) % count_all) for dev_j in range(count_all)))
+    items = tuple(((src_i, to_i) for to_i, src_i in vals))
+    seen_now, value_now = ([], [])
+    h = 0
+    while h < count_all - 1:
+        if h % 2 == 0:
+            seen_now.append(
+                lax.ppermute(seen_now[-1] if seen_now else tokens, axis_name="fsdp", perm=vals)
+            )
+        else:
+            value_now.append(
+                lax.ppermute(value_now[-1] if value_now else tokens, axis_name="fsdp", perm=items)
+            )
+        h += 1
+    view_out = jnp.stack([*seen_now[::-1], tokens, *value_now])
+    mat_out = lax.axis_index("fsdp") - len(seen_now)
+    view_out = view_out[(jnp.arange(count_all) - mat_out) % count_all]
+    group_tokens = wait_gates(view_out, 0)
     group_rows = group_tokens.shape[0]
     local_cols = in_weight.shape[1]
     partial = jnp.dot(

time: 304 us -> 297 us (0.977)
  waiting for transfers between devices: 121 us -> 103 us
  local copies, waits for them, and re-layouts: 31.5 us -> 35.9 us
  starting transfers between devices: 10.2 us -> 14 us
  other arithmetic: 42.7 us -> 46 us
    all_gather x1 -> x0, waiting for transfers between devices: 66.4 us -> none  [shards(): group_tokens = lax.all_gather(tokens, 'fsdp', axis=0, tiled=True)]
    ppermute x0 -> x3, waiting for transfers between devices: none -> 51.3 us  [the longest x2 35.7 us: shards(): lax.ppermute(seen_now[-1] if seen_now else tokens, axis_name='fsdp', perm...]
    gather x0 -> x1, local copies, waits for them, and re-layouts: none -> 4.31 us  [shards(): view_out = view_out[(jnp.arange(count_all) - mat_out) % count_all]]
    ppermute x0 -> x3, starting transfers between devices: none -> 3.83 us  [the longest x1 2.25 us: shards(): lax.ppermute(value_now[-1] if value_now else tokens, axis_name='fsdp', pe...]
    another operation x0 -> x1, other arithmetic: none -> 3.22 us  [shards(): view_out = jnp.stack([*seen_now[::-1], tokens, *value_now])]
  transfers between devices with their start and end apart: 5 -> 7, of which waited for: 2 -> 4; matrix products, arithmetic and copies ran while one was open for 3% -> 3% of each run, Pallas kernels for 0% -> 0%
where the time goes in v1:
time: 297 us; the launch traced here: 295 us
  waiting for transfers between devices  103 us (35%)
  matrix products  52.3 us (18%)
  other arithmetic  46 us (15%)
  local copies, waits for them, and re-layouts  35.9 us (12%)
  blocking collectives  30.4 us (10%)
  starting transfers between devices  14 us (5%)
  between operations  13.5 us (5%)
    all_to_all x1, waiting for transfers between devices, shards(): projected = lax.all_to_all(partial, 'fsdp', 0, 2, tiled=True)  51.6 us
    ppermute x2, waiting for transfers between devices, shards(): lax.ppermute(seen_now[-1] if seen_now else tokens, axis_name='fsdp', perm...  35.7 us
    add x4, other arithmetic, add_block(): return spectrum + packed_product(response[None], signal, block_len)  19.9 us
    all_gather x1, blocking collectives, shards(): lax.all_gather(response_out, 'fsdp', axis=2, tiled=True)  18.5 us
    ppermute x1, waiting for transfers between devices, shards(): lax.ppermute(value_now[-1] if value_now else tokens, axis_name='fsdp', pe...  15.6 us
    all_gather x1, blocking collectives, shards(): lax.all_gather(skip_gain, 'fsdp', axis=0, tiled=True)  11.9 us
    dot_general x4, matrix products, add_block(): jnp.einsum('fc,scd->sfd', forward_half, block_rows.astype(jnp.float32), p...  10.7 us
    dot_general x4, matrix products, kernel_response(): jnp.dot(jnp.dot(forward, paired, precision=lax.Precision.HIGHEST), out_co...  10.3 us
  transfers between devices with their start and end apart: 7, of which 4 were waited for; matrix products, arithmetic and copies ran while one was open for 3% of the time, Pallas kernels for 0%

profile of v1, /device:TPU:2, one launch (start us, length us, event | category | flops | bytes accessed | tf_op | source)
XLA Modules:
  0.0 295.4 jit_solution(6264649592665230180)
XLA Ops:
  6.5 1.6 collective-permute-start
  8.1 2.2 collective-permute-start.2
  10.4 18.8 %collective-permute-done = bf16[2,128,1536]{2,1,0:T(8,128)(2,1)} collective-permute-done((bf16[2,128,1536]{2,1,0:T(8,128)(2,1)}, bf16[2,128,1536]{2,1,0:T(8,128)(2,1)}, u32[]{:S(2)}, u32[]{:S(2)}) %collective-permute-start) | collective-permute-done | bytes 786464 | tf_op jit(solution)/shard_map/ppermute | solution.py:102
  29.1 15.6 %collective-permute-done.2 = bf16[2,128,1536]{2,1,0:T(8,128)(2,1)} collective-permute-done((bf16[2,128,1536]{2,1,0:T(8,128)(2,1)}, bf16[2,128,1536]{2,1,0:T(8,128)(2,1)}, u32[]{:S(2)}, u32[]{:S(2)}) %collective-permute-start.2) | collective-permute-done | bytes 786464 | tf_op jit(solution)/shard_map/ppermute | solution.py:106
  44.8 17.0 %collective-permute-done.1 = bf16[2,128,1536]{2,1,0:T(8,128)(2,1)} collective-permute-done((bf16[2,128,1536]{2,1,0:T(8,128)(2,1)}, bf16[2,128,1536]{2,1,0:T(8,128)(2,1)}, u32[]{:S(2)}, u32[]{:S(2)}) %collective-permute-start.1) | collective-permute-done | bytes 786464 | tf_op jit(solution)/shard_map/ppermute | solution.py:102
  61.7 3.2 %pad_maximum_fusion = bf16[4,2,128,1536]{3,2,1,0:T(8,128)(2,1)} fusion(bf16[1,2,128,1536]{3,2,1,0:T(8,128)(2,1)} %bitcast.3, bf16[1,2,128,1536]{3,2,1,0:T(8,128)(2,1)} %bitcast.71, bf16[1,2,128,1536]{3,2,1,0:T(8,128)(2,1)} %bitcast.1, bf16[1,2,128,1536]{3,2,1,0:T(8,128)(2,1)} %bitcast), kind=kLoop, calls=%fused_computation.60 | loop fusion | flops 4718592 | bytes 6291456 | tf_op jit(solution)/shard_map/stack | solution.py:109
  65.0 4.3 %gather_fusion = bf16[4,2,128,1536]{3,2,1,0:T(8,128)(2,1)} fusion(bf16[4,2,128,1536]{3,2,1,0:T(8,128)(2,1)} %pad_maximum_fusion, s32[1024]{0:T(1024)S(1)} %pad_clamp_fusion), kind=kCustom, calls=%fused_computation | custom fusion | bytes 6291472 | tf_op jit(solution)/shard_map/gather | solution.py:111
  69.3 7.5 %convolution_convert_fusion = bf16[1024,1152]{1,0:T(8,128)(2,1)} fusion(bf16[1024,1536]{1,0:T(8,128)(2,1)} %bitcast.69, bf16[1536,1152]{1,0:T(8,128)(2,1)S(1)} %copy-done), kind=kOutput, calls=%fused_computation.59 | convolution fusion | flops 3625058304 | bytes 9043968 | tf_op jit(solution)/shard_map/dot_general | solution.py:115
  76.8 4.6 %all-to-all-start = ((bf16[8,128,1152]{2,1,0:T(8,128)(2,1)}), bf16[8,128,1152]{2,1,0:T(8,128)(2,1)}, u32[]{:S(2)}, u32[]{:S(2)}) async-start(bf16[8,128,1152]{2,1,0:T(8,128)(2,1)} %bitcast.70), calls=%async_computation | async-start | bytes 4718592 | tf_op jit(solution)/shard_map/all_to_all | solution.py:121
  81.6 51.6 %all-to-all-done = bf16[8,128,1152]{2,1,0:T(8,128)(2,1)} async-done(((bf16[8,128,1152]{2,1,0:T(8,128)(2,1)}), bf16[8,128,1152]{2,1,0:T(8,128)(2,1)}, u32[]{:S(2)}, u32[]{:S(2)}) %all-to-all-start) | async-done | bytes 2359328 | tf_op jit(solution)/shard_map/all_to_all | solution.py:121
  133.2 4.3 %copy.20 = bf16[4,2,128,1152]{2,3,0,1:T(8,128)(2,1)} copy(bf16[4,2,128,1152]{3,2,1,0:T(8,128)(2,1)} %bitcast.7) | data formatting | bytes 4718592 | tf_op jit(solution)/shard_map/all_to_all | solution.py:121
  137.6 5.3 %fusion.58 = (bf16[2,1,4608]{1,2,0:T(8,128)(2,1)}, bf16[2,1,4608]{1,2,0:T(8,128)(2,1)}) fusion(bf16[2,128,4608]{1,2,0:T(8,128)(2,1)} %bitcast.66), kind=kLoop, calls=%fused_computation.120 | loop fusion | bytes 73728 | tf_op jit(solution)/shard_map/slice | solution.py:19
  142.8 2.7 copy.21
  145.5 1.9 collective-permute-start.3
  147.4 2.7 copy.23
  150.1 3.6 %collective-permute-start.4 = (bf16[2,1,4608]{2,0,1:T(2,128)(2,1)}, bf16[2,1,4608]{2,0,1:T(2,128)(2,1)}, u32[]{:S(2)}, u32[]{:S(2)}) collective-permute-start(bf16[2,1,4608]{2,0,1:T(2,128)(2,1)} %copy.23), channel_id=1, source_target_pairs={{4,0},{8,4},{12,8},{5,1},{9,5},{13,9},{6,2},{10,6},{14,10},{7,3},{... | collective-permute-start | bytes 55304 | tf_op jit(solution)/shard_map/ppermute | solution.py:24
  153.8 1.8 slice_reduce_fusion.2
  155.5 2.6 copy.22
  158.2 2.6 copy.24
  160.8 7.7 %multiply_add_fusion = f32[2,128,4608]{1,2,0:T(8,128)S(1)} fusion(bf16[2,128,4608]{1,2,0:T(8,128)(2,1)} %bitcast.67, bf16[2,1,4608]{1,2,0:T(8,128)(2,1)} %copy.24, bf16[2,1,4608]{1,2,0:T(8,128)(2,1)} %copy.22, f32[4608]{0:T(1024)} %get-tuple-element.353, f32[4608]{0:T(1024)} %get-tuple-element.354, f32[4608]{0:T(1024)} %get-tuple-element.352), kind=kLoop, calls=%fused_computation.58 | loop fusion | flops 16515072 | bytes 7170048 | tf_op jit(solution)/shard_map/add | solution.py:124
  168.5 2.1 copy-done.3
  170.6 1.0 fusion.31
  171.7 11.9 %all-gather = f32[4,1,384]{2,1,0:T(1,128)S(1)} all-gather(f32[1,1,384]{2,1,0:T(1,128)S(1)} %reshape.236), channel_id=1, replica_groups=mesh['groups'=2,'seq'=4,'fsdp'=4] {'fsdp'}, dimensions={0}, use_global_device_ids=true | all-gather | bytes 7680 | tf_op jit(solution)/shard_map/all_gather | solution.py:137
  183.6 0.5 negate_select_fusion.2
  184.2 0.7 fusion.36
  184.8 0.7 pad_maximum_fusion.3
  185.6 0.9 select_multiply_fusion.1
  186.5 18.5 %all_gather.9 = f32[2,64,1536]{2,1,0:T(8,128)} all-gather(f32[2,64,384]{2,1,0:T(8,128)} %param.19), channel_id=1, replica_groups=mesh['groups'=2,'seq'=4,'fsdp'=4] {'fsdp'}, dimensions={2}, use_global_device_ids=true | all-gather | bytes 983040 | tf_op jit(solution)/shard_map/all_gather | solution.py:136
  205.1 72.5 %while.16 = (s32[]{:T(128)}, f32[2,256,1536]{2,1,0:T(8,128)}, s32[]{:T(128)}, f32[17,64]{1,0:T(8,128)}, f32[64]{0:T(128)}, /*index=5*/f32[64,64]{1,0:T(8,128)}, ...) while((s32[]{:T(128)}, f32[2,256,1536]{2,1,0:T(8,128)}, ...), condition=%wide.region_1.2_spmd.clone, body=%wide.region_0.1_spmd.clone.sunk | while | flops 1934166400 | bytes 34141608 | solution.py:182
  205.4 1.2 fusion.94
  206.6 1.2 broadcast_multiply_fusion.3
  207.8 1.3 fusion.95
  209.2 2.6 convolution_bitcast_fusion.6
  211.8 1.3 slice_bitcast_fusion.3
  213.0 2.7 convolution_bitcast_fusion.5
  215.7 2.5 select_subtract_fusion.2
  218.2 4.3 %maximum_add_fusion.2 = f32[2,256,1536]{2,1,0:T(8,128)} fusion(f32[2,128,1536]{2,1,0:T(8,128)} %get-tuple-element.484, f32[2,128,1536]{2,1,0:T(8,128)} %get-tuple-element.485, f32[2,256,1536]{2,1,0:T(8,128)} %get-tuple-element.502, pred[]{:T(512)S(6)} %compare.14), kind=kLoop, calls=%fused_computation.3.clone.1 | loop fusion | flops 2359296 | bytes 9437185 | tf_op jit(solution)/shard_map/while/body/eval_jaxpr/add | solution.py:171
  222.8 1.2 fusion.94
  224.0 1.2 broadcast_multiply_fusion.3
  225.2 1.3 fusion.95
  226.6 2.6 convolution_bitcast_fusion.6
  229.1 1.3 slice_bitcast_fusion.3
  230.4 2.7 convolution_bitcast_fusion.5
  233.1 2.5 select_subtract_fusion.2
  235.6 5.2 %maximum_add_fusion.2 = f32[2,256,1536]{2,1,0:T(8,128)} fusion(f32[2,128,1536]{2,1,0:T(8,128)} %get-tuple-element.484, f32[2,128,1536]{2,1,0:T(8,128)} %get-tuple-element.485, f32[2,256,1536]{2,1,0:T(8,128)} %get-tuple-element.502, pred[]{:T(512)S(6)} %compare.14), kind=kLoop, calls=%fused_computation.3.clone.1 | loop fusion | flops 2359296 | bytes 9437185 | tf_op jit(solution)/shard_map/while/body/eval_jaxpr/add | solution.py:171
  240.9 0.2 fusion.93
  241.1 1.2 fusion.94
  242.3 1.2 broadcast_multiply_fusion.3
  243.6 1.3 fusion.95
  244.9 2.6 convolution_bitcast_fusion.6
  247.5 1.3 slice_bitcast_fusion.3
  248.8 2.7 convolution_bitcast_fusion.5
  251.5 2.5 select_subtract_fusion.2
  254.0 5.2 %maximum_add_fusion.2 = f32[2,256,1536]{2,1,0:T(8,128)} fusion(f32[2,128,1536]{2,1,0:T(8,128)} %get-tuple-element.484, f32[2,128,1536]{2,1,0:T(8,128)} %get-tuple-element.485, f32[2,256,1536]{2,1,0:T(8,128)} %get-tuple-element.502, pred[]{:T(512)S(6)} %compare.14), kind=kLoop, calls=%fused_computation.3.clone.1 | loop fusion | flops 2359296 | bytes 9437185 | tf_op jit(solution)/shard_map/while/body/eval_jaxpr/add | solution.py:171
  259.5 1.2 fusion.94
  260.7 1.2 broadcast_multiply_fusion.3
  261.9 1.3 fusion.95
  263.3 2.6 convolution_bitcast_fusion.6
  265.9 1.3 slice_bitcast_fusion.3
  267.1 2.7 convolution_bitcast_fusion.5
  269.8 2.5 select_subtract_fusion.2
  272.3 5.2 %maximum_add_fusion.2 = f32[2,256,1536]{2,1,0:T(8,128)} fusion(f32[2,128,1536]{2,1,0:T(8,128)} %get-tuple-element.484, f32[2,128,1536]{2,1,0:T(8,128)} %get-tuple-element.485, f32[2,256,1536]{2,1,0:T(8,128)} %get-tuple-element.502, pred[]{:T(512)S(6)} %compare.14), kind=kLoop, calls=%fused_computation.3.clone.1 | loop fusion | flops 2359296 | bytes 9437185 | tf_op jit(solution)/shard_map/while/body/eval_jaxpr/add | solution.py:171
  277.5 8.8 %fusion.32 = bf16[2,128,1536]{1,2,0:T(8,128)(2,1)} fusion(f32[2,128,4608]{1,2,0:T(8,128)} %copy-done.3, f32[2,256,1536]{2,1,0:T(8,128)} %get-tuple-element.280, bf16[2,128,1536]{1,2,0:T(8,128)(2,1)} %fusion.31, f32[1536]{0:T(1024)S(1)} %reshape.237, f32[128,128]{1,0:T(8,128)} %get-tuple-element.392, f32[128,128]{1,0:T(8,128)} %get-tuple-element.391), kind=kOutput, calls=%fused_computation.69 | convolution fusion | flops 1209958400 | bytes 6428672 | tf_op jit(solution)/shard_map/if,sfd->sid/dot_general | solution.py:183
  286.3 2.3 copy.27
  (66 shorter events, 1.2 us)
Async XLA Ops:
  6.5 62.7 %copy-start = (bf16[1536,1152]{1,0:T(8,128)(2,1)S(1)}, bf16[1536,1152]{1,0:T(8,128)(2,1)}, u32[]{:S(2)}) copy-start(bf16[1536,1152]{1,0:T(8,128)(2,1)} %param.13) | copy-start | bytes 10616836
  6.5 22.6 %collective-permute-start = (bf16[2,128,1536]{2,1,0:T(8,128)(2,1)}, bf16[2,128,1536]{2,1,0:T(8,128)(2,1)}, u32[]{:S(2)}, u32[]{:S(2)}) collective-permute-start(bf16[2,128,1536]{2,1,0:T(8,128)(2,1)} %param.12), channel_id=1, source_target_pairs={{0,1},{1,2},{2,3},{3,0},{4,5},{5,6},{6,7},{7,4},{8,9},{9,10},{10,1... | collective-permute-start | bytes 2359304 | tf_op jit(solution)/shard_map/ppermute | solution.py:102
  8.1 36.6 %collective-permute-start.2 = (bf16[2,128,1536]{2,1,0:T(8,128)(2,1)}, bf16[2,128,1536]{2,1,0:T(8,128)(2,1)}, u32[]{:S(2)}, u32[]{:S(2)}) collective-permute-start(bf16[2,128,1536]{2,1,0:T(8,128)(2,1)} %param.12), channel_id=1, source_target_pairs={{1,0},{2,1},{3,2},{0,3},{5,4},{6,5},{7,6},{4,7},{9,8},{10,9},{11,1... | collective-permute-start | bytes 2359304 | tf_op jit(solution)/shard_map/ppermute | solution.py:106
  29.1 32.6 %collective-permute-start.1 = (bf16[2,128,1536]{2,1,0:T(8,128)(2,1)}, bf16[2,128,1536]{2,1,0:T(8,128)(2,1)}, u32[]{:S(2)}, u32[]{:S(2)}) collective-permute-start(bf16[2,128,1536]{2,1,0:T(8,128)(2,1)} %collective-permute-done), channel_id=1, source_target_pairs={{0,1},{1,2},{2,3},{3,0},{4,5},{5,6},{6,7},{7,4},{8,9},{9,10},{10,1... | collective-permute-start | bytes 2359304 | tf_op jit(solution)/shard_map/ppermute | solution.py:102
  76.8 4.7 %copy-start.5 = (s32[2,1]{0,1:T(1,128)S(1)}, s32[2,1]{0,1:T(1,128)}, u32[]{:S(2)}) copy-start(s32[2,1]{0,1:T(1,128)} %param.21) | copy-start | bytes 28
  76.8 56.4 %all-to-all-start = ((bf16[8,128,1152]{2,1,0:T(8,128)(2,1)}), bf16[8,128,1152]{2,1,0:T(8,128)(2,1)}, u32[]{:S(2)}, u32[]{:S(2)}) async-start(bf16[8,128,1152]{2,1,0:T(8,128)(2,1)} %bitcast.70), calls=%async_computation | async-start | bytes 4718592 | tf_op jit(solution)/shard_map/all_to_all | solution.py:121
  81.5 123.6 %all-gather.3.cloned.1.call-start = ((), (), s32[]{:S(2)}) async-start(), calls=%async_computation.1 | async-start | bytes 3932160 | tf_op jit(solution)/shard_map/all_gather | solution.py:174
  145.5 10.0 %collective-permute-start.3 = (bf16[2,1,4608]{2,0,1:T(2,128)(2,1)}, bf16[2,1,4608]{2,0,1:T(2,128)(2,1)}, u32[]{:S(2)}, u32[]{:S(2)}) collective-permute-start(bf16[2,1,4608]{2,0,1:T(2,128)(2,1)} %copy.21), channel_id=1, source_target_pairs={{0,4},{4,8},{8,12},{1,5},{5,9},{9,13},{2,6},{6,10},{10,14},{3,7},{... | collective-permute-start | bytes 55304 | tf_op jit(solution)/shard_map/ppermute | solution.py:22
  150.1 8.0 %collective-permute-start.4 = (bf16[2,1,4608]{2,0,1:T(2,128)(2,1)}, bf16[2,1,4608]{2,0,1:T(2,128)(2,1)}, u32[]{:S(2)}, u32[]{:S(2)}) collective-permute-start(bf16[2,1,4608]{2,0,1:T(2,128)(2,1)} %copy.23), channel_id=1, source_target_pairs={{4,0},{8,4},{12,8},{5,1},{9,5},{13,9},{6,2},{10,6},{14,10},{7,3},{... | collective-permute-start | bytes 55304 | tf_op jit(solution)/shard_map/ppermute | solution.py:24
  168.5 2.1 copy-start.3
  170.6 1.1 copy-start.4
  213.0 2.7 copy-start.1
  213.0 2.7 copy-start.2
  230.4 2.7 copy-start.1
  230.4 2.7 copy-start.2
  248.8 2.7 copy-start.1
  248.8 2.7 copy-start.2
  267.1 2.7 copy-start.1
  267.1 2.7 copy-start.2
Sparse Core Ops, SparseCore 0:
  171.8 26.8 all-gather.2
